TPU v7x, 32 devices: a whole 2x2x4 slice. The times are simulated.
32 devices in a mesh: seq: 8 (over z, y), fsdp: 4 (over x, core).
Axes of the slice: x: 2, y: 2, z: 4, core: 2. Of those that a mesh axis runs over, the one named last changes fastest.
Arguments:
- tokens: bfloat16 [2048, 2048], P('seq', 'fsdp'), may hold values from -6 to 6
- deal_order: int32 [8, 8], replicated, may hold values from 0 to 7, each once within a row
- lengths: int32 [4], replicated, may hold values from 1 to 1024, 2048 in all
- x_weight: bfloat16 [2048, 1536], P(None, 'fsdp'), may hold values from -0.0390625 to 0.0390625
- z_weight: bfloat16 [2048, 1536], P(None, 'fsdp'), may hold values from -0.125 to 0.125
- shared_weight: bfloat16 [2048, 512], P('fsdp'), may hold values from -0.0390625 to 0.0390625
- step_weight: bfloat16 [2048, 24], P(None, 'fsdp'), may hold values from -0.125 to 0.125
- conv_heads: float32 [4, 1536], P(None, 'fsdp'), may hold values from -3 to 3
- conv_shared: float32 [4, 512], replicated, may hold values from -3 to 3
- step_bias: float32 [24], P('fsdp'), as said below
- decay_log: float32 [24], P('fsdp'), may hold values from -7.1 to -2.8, as said below
- skip_gain: float32 [24], P('fsdp'), may hold values from 0.5 to 1.5
Outputs:
- mixed: bfloat16 [2048, 1536], P('seq', 'fsdp')
Inputs may be any that keep to these rules, and one draw needn't show every extreme that they name: `deal_order`: each row is a permutation of 0 to 7. The lengths sum to 2048. `decay_log`: one value a head. `step_bias`: one value a head.
All inputs are finite; a program needn't handle non-finite values.
Results may differ from a plain program's by a relative error of at most 0.0095.
Values may be sent and summed in bfloat16 or wider, within the bound.
No kernel may reach another device: no remote copies, remote signals or barrier semaphores. Data moves between devices by JAX's collectives and lax.ppermute only.
A program may use at most 128 MiB of HBM per device.

v0:
```python
import jax
import jax.numpy as jnp
from jax import lax
from jax.sharding import PartitionSpec as P

precise = lax.Precision.HIGHEST


def shifted(array, axis, by):
    count = lax.axis_size(axis)
    pairs = [(i, i + by) for i in range(count) if 0 <= i + by < count]
    return lax.ppermute(array, axis, pairs)


def prefix(part, axis, combine, identity):
    place = lax.axis_index(axis)
    gathered = jax.tree.map(lambda a: lax.all_gather(a, axis), part)
    state = jax.tree.map(lambda a, e: jnp.zeros_like(a) + jnp.asarray(e, a.dtype), part, identity)

    def one(turn, state):
        return combine(
            state, jax.tree.map(lambda a: lax.dynamic_index_in_dim(a, turn, 0, False), gathered)
        )

    return lax.fori_loop(0, place, one, state)


def segment_of(positions, lengths):
    prompt_ends = jnp.cumsum(lengths)
    counted = (positions[:, None] >= prompt_ends[None, :]).astype(jnp.int32)
    return jnp.sum(counted, axis=1)


def causal_conv(extended, segment_ids, weights, conv_width):
    out_rows = extended.shape[0] - conv_width + 1
    target = segment_ids[conv_width - 1 :]
    running = jnp.zeros((out_rows, extended.shape[1]), jnp.float32)
    for tap_index in range(conv_width):
        matched = (segment_ids[tap_index : tap_index + out_rows] == target).astype(jnp.float32)
        running = (
            running
            + weights[tap_index][None, :]
            * extended[tap_index : tap_index + out_rows]
            * matched[:, None]
        )
    return running


def local_terms(x_heads, b_rows, c_rows, step_size, decay_log, segment_ids, seg_before):
    log_decay = -jnp.exp(decay_log)[None, :] * step_size
    cum_decay = jnp.cumsum(log_decay, axis=0)
    positions_in = jnp.arange(x_heads.shape[0], dtype=jnp.int32)
    same_prompt = (segment_ids[:, None] == segment_ids[None, :]) & (
        positions_in[:, None] >= positions_in[None, :]
    )
    decay_gap = cum_decay.T[:, :, None] - cum_decay.T[:, None, :]
    decay_matrix = jnp.exp(jnp.where(same_prompt[None], decay_gap, -jnp.inf))
    scores = jnp.dot(c_rows, b_rows.T, precision=precise)
    x_step = x_heads * step_size[:, :, None]
    intra = jnp.einsum("hts,shp->thp", scores[None] * decay_matrix, x_step, precision=precise)
    to_end = jnp.exp(
        jnp.where(
            (segment_ids == segment_ids[-1])[:, None], cum_decay[-1][None, :] - cum_decay, -jnp.inf
        )
    )
    state_out = jnp.einsum("shp,sn->hpn", x_step * to_end[:, :, None], b_rows, precision=precise)
    carried = segment_ids == seg_before
    carry_in = jnp.exp(jnp.where(carried[:, None], cum_decay, -jnp.inf))
    block_decay = jnp.where(carried[-1], jnp.exp(cum_decay[-1]), 0.0)
    return (intra, state_out, carry_in, block_decay)


def combine(earlier, later):
    return (earlier[0] * later[0], later[0][:, None, None] * earlier[1] + later[1])


def per_device(
    tokens,
    deal_order,
    lengths,
    x_weight,
    z_weight,
    shared_weight,
    step_weight,
    conv_heads,
    conv_shared,
    step_bias,
    decay_log,
    skip_gain,
):
    seq_count = lax.axis_size("seq")
    own_index = lax.axis_index("seq")
    tok_dev = tokens.shape[0]
    piece_rows = tok_dev // seq_count
    slot_rows = tokens.reshape(seq_count, piece_rows, tokens.shape[1])
    arrived = lax.all_to_all(slot_rows, "seq", split_axis=0, concat_axis=0, tiled=True)
    dealt_row = lax.dynamic_slice_in_dim(deal_order, own_index, 1, 0)[0]
    inverse = jnp.argsort(dealt_row)
    stream_block = jnp.take(arrived, inverse, axis=0).reshape(tok_dev, tokens.shape[1])
    inner_dev = x_weight.shape[1]
    heads_dev = step_weight.shape[1]
    head_dim = inner_dev // heads_dev
    state_dim = shared_weight.shape[1] // 2
    w_full = lax.all_gather(shared_weight, "fsdp", axis=0, tiled=True)
    weight_list = (x_weight, z_weight, step_weight, w_full)
    feature_part = lax.all_gather(stream_block, "fsdp", axis=1, tiled=True)
    x_acc, z_acc, step_acc, bc_acc = tuple(
        (
            jnp.dot(feature_part, weight, preferred_element_type=jnp.float32)
            for weight in weight_list
        )
    )
    x_raw = x_acc.astype(jnp.bfloat16)
    z_raw = z_acc.astype(jnp.bfloat16)
    bc_raw = bc_acc.astype(jnp.bfloat16)
    step_size = jax.nn.softplus(step_acc + step_bias[None, :])
    mixed_in = jnp.concatenate([x_raw, bc_raw], axis=1)
    conv_width = conv_heads.shape[0]
    prior_rows = shifted(mixed_in[tok_dev - conv_width + 1 :], "seq", 1)
    first_pos = own_index * tok_dev
    positions = first_pos - (conv_width - 1) + jnp.arange(tok_dev + conv_width - 1, dtype=jnp.int32)
    seg_ext = segment_of(positions, lengths)
    extended = jnp.concatenate([prior_rows, mixed_in], axis=0).astype(jnp.float32)
    activated = jax.nn.silu(
        causal_conv(
            extended, seg_ext, jnp.concatenate([conv_heads, conv_shared], axis=1), conv_width
        )
    )
    segment_ids = seg_ext[conv_width - 1 :]
    seg_before = jnp.where(own_index == 0, -1, seg_ext[conv_width - 2])
    x_heads = activated[:, :inner_dev].reshape(tok_dev, heads_dev, head_dim)
    b_rows = activated[:, inner_dev : inner_dev + state_dim]
    c_rows = activated[:, inner_dev + state_dim :]
    intra, state_out, carry_in, block_decay = local_terms(
        x_heads, b_rows, c_rows, step_size, decay_log, segment_ids, seg_before
    )
    identity = (jnp.ones_like(block_decay), jnp.zeros_like(state_out))
    _, state_in = prefix((block_decay, state_out), "seq", combine, identity)
    incoming = jnp.einsum("tn,hpn->thp", c_rows, state_in, precision=precise)
    y_block = intra + carry_in[:, :, None] * incoming + skip_gain[None, :, None] * x_heads
    gated = (y_block.reshape(tok_dev, inner_dev) * jax.nn.silu(z_raw.astype(jnp.float32))).astype(
        jnp.bfloat16
    )
    ordered = gated.reshape(seq_count, piece_rows, inner_dev)
    outgoing = jnp.take(ordered, dealt_row, axis=0)
    returned = lax.all_to_all(outgoing, "seq", split_axis=0, concat_axis=0, tiled=True)
    return returned.reshape(tok_dev, inner_dev)


def solution(mesh):
    return jax.shard_map(
        per_device,
        mesh=mesh,
        in_specs=(
            P("seq", "fsdp"),
            P(),
            P(),
            P(None, "fsdp"),
            P(None, "fsdp"),
            P("fsdp", None),
            P(None, "fsdp"),
            P(None, "fsdp"),
            P(),
            P("fsdp"),
            P("fsdp"),
            P("fsdp"),
        ),
        out_specs=P("seq", "fsdp"),
        check_vma=False,
    )
```

profile of v0, /device:TPU:0, one launch (start us, length us, event | category | flops | bytes accessed | tf_op | source)
XLA Modules:
  0.0 173.2 jit_solution(6664324433288918847)
XLA Ops:
  6.6 7.4 %all-to-all-start = ((bf16[8,32,512]{2,1,0:T(8,128)(2,1)}), bf16[8,32,512]{2,1,0:T(8,128)(2,1)S(1)}, u32[]{:S(2)}, u32[]{:S(2)}) async-start(bf16[8,32,512]{2,1,0:T(8,128)(2,1)} %bitcast.90), calls=%async_computation | async-start | bytes 524288 | tf_op jit(solution)/shard_map/all_to_all | solution.py:96
  14.0 1.3 compare_and_fusion.1
  15.3 1.0 sort.17
  16.5 6.5 %all-to-all-done = bf16[8,32,512]{2,1,0:T(8,128)(2,1)S(1)} async-done(((bf16[8,32,512]{2,1,0:T(8,128)(2,1)}), bf16[8,32,512]{2,1,0:T(8,128)(2,1)S(1)}, u32[]{:S(2)}, u32[]{:S(2)}) %all-to-all-start) | async-done | bytes 262176 | tf_op jit(solution)/shard_map/all_to_all | solution.py:96
  22.9 0.6 gather_fusion
  23.5 0.8 bitcast_select_fusion
  24.4 0.7 all-gather.8.cloned.1.call-update
  25.4 0.6 fusion.51
  26.6 0.7 broadcast_compare_fusion
  27.4 0.6 slice.89
  28.0 12.2 %all-gather.6.cloned.1.call-done = bf16[256,2048]{1,0:T(8,128)(2,1)} async-done(((bf16[256,512]{1,0:T(8,128)(2,1)}), bf16[256,2048]{1,0:T(8,128)(2,1)}) %all-gather.6.cloned.1.call-update) | async-done | bytes 1048592 | tf_op jit(solution)/shard_map/all_gather | solution.py:106
  40.3 1.6 fusion.41
  41.9 1.8 %reduce-window.19 = f32[6,2,128]{2,1,0:T(2,128)S(1)} reduce-window(f32[6,2,128]{2,1,0:T(2,128)S(1)} %reshape.175, f32[]{:T(128)} %constant.76.clone.1), window={size=1x1x128 pad=0_0x0_0x127_0}, to_apply=%region_3.4 | reduce-window | flops 195072 | bytes 12292 | tf_op jit(solution)/shard_map/reduce-window.1
  44.2 0.8 slice_reduce_fusion
  45.1 1.9 %convolution_convert_fusion.2 = bf16[256,384]{1,0:T(8,128)(2,1)S(1)} fusion(bf16[256,2048]{1,0:T(8,128)(2,1)} %all-gather.6.cloned.1.call-done, bf16[2048,384]{1,0:T(8,128)(2,1)S(1)} %copy-done), kind=kOutput, calls=%fused_computation.16 | convolution fusion | flops 402751488 | bytes 2818048 | tf_op jit(solution)/shard_map/dot_general | solution.py:109
  47.0 17.4 %all-gather.8.cloned.1.call-done = bf16[2048,512]{1,0:T(8,128)(2,1)} async-done(((bf16[512,512]{1,0:T(8,128)(2,1)}), bf16[2048,512]{1,0:T(8,128)(2,1)}) %all-gather.8.cloned.1.call-update) | async-done | bytes 2097168 | tf_op jit(solution)/shard_map/all_gather | solution.py:104
  64.5 2.3 %convolution_convert_fusion = bf16[256,512]{1,0:T(8,128)(2,1)S(1)} fusion(bf16[256,2048]{1,0:T(8,128)(2,1)S(1)} %copy-done.1, bf16[2048,512]{1,0:T(8,128)(2,1)} %all-gather.8.cloned.1.call-done), kind=kOutput, calls=%fused_computation.12 | convolution fusion | flops 537001984 | bytes 3407872 | tf_op jit(solution)/shard_map/dot_general | solution.py:109
  66.8 3.4 %collective-permute-start = (bf16[3,896]{1,0:T(4,128)(2,1)S(1)}, bf16[3,896]{1,0:T(4,128)(2,1)S(1)}, u32[]{:S(2)}, u32[]{:S(2)}) collective-permute-start(bf16[3,896]{1,0:T(4,128)(2,1)S(1)} %pad_maximum_fusion), channel_id=1, source_target_pairs={{0,4},{4,8},{8,12},{12,16},{16,20},{20,24},{24,28},{1,5},{5,9},{9,... | collective-permute-start | bytes 16136 | tf_op jit(solution)/shard_map/ppermute | solution.py:12
  70.2 1.3 collective-permute-done
  71.6 0.7 divide_multiply_fusion
  72.5 1.2 fusion.26
  73.8 0.7 fusion.47
  74.5 0.6 pad_clamp_fusion
  75.1 0.7 fusion.32
  75.9 21.6 %all-gather.1 = f32[8,1,6]{2,1,0:T(1,128)} all-gather(f32[1,1,6]{2,1,0:T(1,128)S(1)} %bitcast.96), channel_id=1, replica_groups=mesh['seq'=8,'fsdp'=4] {'seq'}, dimensions={0}, use_global_device_ids=true | all-gather | bytes 216 | tf_op jit(solution)/shard_map/all_gather | solution.py:17
  97.9 37.2 %all-gather.10.cloned.1.call-done = f32[48,64,256]{2,1,0:T(8,128)} async-done(((f32[6,64,256]{2,1,0:T(8,128)}), f32[48,64,256]{2,1,0:T(8,128)}) %all-gather.10.cloned.1.call-update) | async-done | bytes 3145744 | tf_op jit(solution)/shard_map/all_gather | solution.py:17
  135.2 0.5 convolution_multiply_fusion
  135.7 2.8 %fusion.11 = f32[256,6,64]{0,2,1:T(8,128)S(1)} fusion(f32[256,6,64]{0,2,1:T(8,128)S(1)} %convolution_multiply_fusion, f32[6,256]{1,0:T(8,128)} %bitcast.93, f32[256,256]{1,0:T(8,128)S(1)} %fusion.34, pred[256,256]{1,0:T(8,128)(4,1)} %fusion.32, f32[256,6,64]{0,2,1:T(8,128)S(1)} %bitcast.86, f32[6]{0:T(128)} %param.25, f32[256,6]{0,1:T(8,128)S(1)} %compare_select_fusion.1), kind=kOutput, calls=%fused_computation.11 | convolution fusion | flops 303562752 | bytes 1519640 | tf_op jit(solution)/shard_map/hts,shp->thp/dot_general | solution.py:60
  138.7 2.5 %multiply_convert_fusion = bf16[256,384]{1,0:T(8,128)(2,1)S(1)} fusion(f32[256,384]{1,0:T(8,128)S(1)} %copy.49, bf16[256,2048]{1,0:T(8,128)(2,1)} %all-gather.6.cloned.1.call-done, bf16[2048,384]{1,0:T(8,128)(2,1)} %param.18), kind=kOutput, calls=%fused_computation.35 | convolution fusion | flops 403439616 | bytes 3211264 | tf_op jit(solution)/shard_map/dot_general | solution.py:109
  141.2 0.7 gather_fusion.1
  142.0 24.0 %all_to_all.10 = bf16[8,32,384]{2,1,0:T(8,128)(2,1)S(1)} all-to-all(bf16[8,32,384]{2,1,0:T(8,128)(2,1)S(1)} %broadcast_select_fusion), channel_id=1, replica_groups=mesh['seq'=8,'fsdp'=4] {'seq'}, dimensions={0} | all-to-all | bytes 393216 | tf_op jit(solution)/shard_map/all_to_all | solution.py:146
  166.0 0.7 copy.67
  (58 shorter events, 2.3 us)
Async XLA Ops:
  6.5 38.6 %copy-start = (bf16[2048,384]{1,0:T(8,128)(2,1)S(1)}, bf16[2048,384]{1,0:T(8,128)(2,1)}, u32[]{:S(2)}) copy-start(bf16[2048,384]{1,0:T(8,128)(2,1)} %param.17) | copy-start | bytes 4718596
  6.5 18.6 %copy-start.8 = (s32[4]{0:T(128)S(1)}, s32[4]{0:T(128)}, u32[]{:S(2)}) copy-start(s32[4]{0:T(128)} %param.16) | copy-start | bytes 52
  6.5 21.4 %copy-start.5 = (f32[4,384]{1,0:T(4,128)S(1)}, f32[4,384]{1,0:T(4,128)}, u32[]{:S(2)}) copy-start(f32[4,384]{1,0:T(4,128)} %param.21) | copy-start | bytes 18436
  6.5 21.4 %copy-start.4 = (f32[4,512]{1,0:T(4,128)S(1)}, f32[4,512]{1,0:T(4,128)}, u32[]{:S(2)}) copy-start(f32[4,512]{1,0:T(4,128)} %param.22) | copy-start | bytes 24580
  6.5 21.5 %copy-start.9 = (f32[6]{0:T(128)S(1)}, f32[6]{0:T(128)}, u32[]{:S(2)}) copy-start(f32[6]{0:T(128)} %param.24) | copy-start | bytes 76
  6.5 33.7 %copy-start.2 = (bf16[2048,6]{0,1:T(8,128)(2,1)S(1)}, bf16[2048,6]{0,1:T(8,128)(2,1)}, u32[]{:S(2)}) copy-start(bf16[2048,6]{0,1:T(8,128)(2,1)} %param.20) | copy-start | bytes 73732
  6.6 33.7 %copy-start.7 = (f32[6]{0:T(128)S(1)}, f32[6]{0:T(128)}, u32[]{:S(2)}) copy-start(f32[6]{0:T(128)} %param.23) | copy-start | bytes 76
  6.6 16.3 %all-to-all-start = ((bf16[8,32,512]{2,1,0:T(8,128)(2,1)}), bf16[8,32,512]{2,1,0:T(8,128)(2,1)S(1)}, u32[]{:S(2)}, u32[]{:S(2)}) async-start(bf16[8,32,512]{2,1,0:T(8,128)(2,1)} %bitcast.90), calls=%async_computation | async-start | bytes 524288 | tf_op jit(solution)/shard_map/all_to_all | solution.py:96
  14.0 26.3 %all-gather.6.cloned.1.call-start = ((), (), s32[]{:S(2)}) async-start(), calls=%async_computation.2 | async-start | bytes 1310720 | tf_op jit(solution)/shard_map/all_gather | solution.py:106
  24.3 40.1 %all-gather.8.cloned.1.call-start = ((), (), s32[]{:S(2)}) async-start(), calls=%async_computation.3 | async-start | bytes 2621440 | tf_op jit(solution)/shard_map/all_gather | solution.py:104
  25.1 110.1 %all-gather.10.cloned.1.call-start = ((), (), s32[]{:S(2)}) async-start(), calls=%async_computation.4 | async-start | bytes 3538944 | tf_op jit(solution)/shard_map/all_gather | solution.py:17
  41.9 22.5 %copy-start.1 = (bf16[256,2048]{1,0:T(8,128)(2,1)S(1)}, bf16[256,2048]{1,0:T(8,128)(2,1)}, u32[]{:S(2)}) copy-start(bf16[256,2048]{1,0:T(8,128)(2,1)} %all-gather.6.cloned.1.call-done) | copy-start | bytes 3145732
  44.2 0.8 copy-start.3
  66.8 4.7 %collective-permute-start = (bf16[3,896]{1,0:T(4,128)(2,1)S(1)}, bf16[3,896]{1,0:T(4,128)(2,1)S(1)}, u32[]{:S(2)}, u32[]{:S(2)}) collective-permute-start(bf16[3,896]{1,0:T(4,128)(2,1)S(1)} %pad_maximum_fusion), channel_id=1, source_target_pairs={{0,4},{4,8},{8,12},{12,16},{16,20},{20,24},{24,28},{1,5},{5,9},{9,... | collective-permute-start | bytes 16136 | tf_op jit(solution)/shard_map/ppermute | solution.py:12
  138.7 3.2 %copy-start.6 = (pred[8]{0:T(512)(128)(4,1)S(1)}, pred[8]{0:T(512)(128)(4,1)}, u32[]{:S(2)}) copy-start(pred[8]{0:T(512)(128)(4,1)} %get-tuple-element.68) | copy-start | bytes 28
Sparse Core Ops, SparseCore 0:
  24.5 15.7 all-gather.5
  41.8 22.5 all-gather.7
  73.9 61.2 all-gather.9
where the time goes:
time: 174 us; the launch traced here: 173 us
  waiting for transfers between devices  75.4 us (43%)
  blocking collectives  45.7 us (26%)
  between operations  14 us (8%)
  matrix products  13.3 us (8%)
  starting transfers between devices  10.9 us (6%)
  other arithmetic  9.84 us (6%)
  local copies, waits for them, and re-layouts  4.14 us (2%)
    all_gather x1, waiting for transfers between devices, prefix(): gathered = jax.tree.map(lambda a: lax.all_gather(a, axis), part)  37.2 us
    all_to_all x1, blocking collectives, per_device(): lax.all_to_all(outgoing, 'seq', split_axis=0, concat_axis=0, tiled=True)  24 us
    all_gather x1, blocking collectives, prefix(): gathered = jax.tree.map(lambda a: lax.all_gather(a, axis), part)  21.6 us
    all_gather x1, waiting for transfers between devices, per_device(): w_full = lax.all_gather(shared_weight, 'fsdp', axis=0, tiled=True)  17.4 us
    all_gather x1, waiting for transfers between devices, per_device(): feature_part = lax.all_gather(stream_block, 'fsdp', axis=1, tiled=True)  12.2 us
    dot_general x4, matrix products, per_device(): jnp.dot(feature_part, weight, preferred_element_type=jnp.float32)  8.34 us
    all_to_all x1, starting transfers between devices, per_device(): lax.all_to_all(slot_rows, 'seq', split_axis=0, concat_axis=0, tiled=True)  7.42 us
    all_to_all x1, waiting for transfers between devices, per_device(): lax.all_to_all(slot_rows, 'seq', split_axis=0, concat_axis=0, tiled=True)  6.45 us
  transfers between devices with their start and end apart: 5, of which 5 were waited for; matrix products, arithmetic and copies ran while one was open for 8% of the time, Pallas kernels for 0%

commit v1 on v0

--- a/solution.py
+++ b/solution.py
@@ -101,7 +101,12 @@
     heads_dev = step_weight.shape[1]
     head_dim = inner_dev // heads_dev
     state_dim = shared_weight.shape[1] // 2
-    w_full = lax.all_gather(shared_weight, "fsdp", axis=0, tiled=True)
+    ring = [shared_weight]
+    for hop in range(3):
+        ring.append(lax.ppermute(ring[-1], "fsdp", [(dev, (dev + 1) % 4) for dev in range(4)]))
+    w_full = jnp.roll(
+        jnp.concatenate(ring[::-1], axis=0), (lax.axis_index("fsdp") + 1) * ring[0].shape[0], axis=0
+    )
     weight_list = (x_weight, z_weight, step_weight, w_full)
     feature_part = lax.all_gather(stream_block, "fsdp", axis=1, tiled=True)
     x_acc, z_acc, step_acc, bc_acc = tuple(

time: 174 us -> 167 us (0.960)
  waiting for transfers between devices: 75.4 us -> 59.6 us
  local copies, waits for them, and re-layouts: 4.14 us -> 13.2 us
  blocking collectives: 45.7 us -> 43.6 us
    ppermute x0 -> x3, waiting for transfers between devices: none -> 21.2 us  [per_device(): lax.ppermute(ring[-1], 'fsdp', [(dev, (dev + 1) % 4) for dev in range(4)])]
    all_gather x1 -> x0, waiting for transfers between devices: 17.4 us -> none  [per_device(): w_full = lax.all_gather(shared_weight, 'fsdp', axis=0, tiled=True)]
    all_gather x1, waiting for transfers between devices: 12.2 us -> 0.01 us  [per_device(): feature_part = lax.all_gather(stream_block, 'fsdp', axis=1, tiled=True)]
    unnamed x23 -> x24, local copies, waits for them, and re-layouts: 0.72 us -> 7.27 us
    all_to_all x1, waiting for transfers between devices: 6.45 us -> 0.1 us  [per_device(): lax.all_to_all(slot_rows, 'seq', split_axis=0, concat_axis=0, tiled=True)]
    all_gather x1, blocking collectives: 21.6 us -> 19.7 us  [prefix(): gathered = jax.tree.map(lambda a: lax.all_gather(a, axis), part)]
  transfers between devices with their start and end apart: 5 -> 7, of which waited for: 5 -> 5; matrix products, arithmetic and copies ran while one was open for 8% -> 14% of each run, Pallas kernels for 0% -> 0%
where the time goes in v1:
time: 167 us; the launch traced here: 166 us
  waiting for transfers between devices  59.6 us (36%)
  blocking collectives  43.6 us (26%)
  between operations  14.3 us (9%)
  local copies, waits for them, and re-layouts  13.2 us (8%)
  matrix products  12.4 us (7%)
  starting transfers between devices  11.4 us (7%)
  other arithmetic  11 us (7%)
    all_gather x1, waiting for transfers between devices, prefix(): gathered = jax.tree.map(lambda a: lax.all_gather(a, axis), part)  38.3 us
    all_to_all x1, blocking collectives, per_device(): lax.all_to_all(outgoing, 'seq', split_axis=0, concat_axis=0, tiled=True)  23.9 us
    ppermute x3, waiting for transfers between devices, per_device(): lax.ppermute(ring[-1], 'fsdp', [(dev, (dev + 1) % 4) for dev in range(4)])  21.2 us
    all_gather x1, blocking collectives, prefix(): gathered = jax.tree.map(lambda a: lax.all_gather(a, axis), part)  19.7 us
    dot_general x4, matrix products, per_device(): jnp.dot(feature_part, weight, preferred_element_type=jnp.float32)  7.53 us
    all_to_all x1, starting transfers between devices, per_device(): lax.all_to_all(slot_rows, 'seq', split_axis=0, concat_axis=0, tiled=True)  7.41 us
    unnamed x24, local copies, waits for them, and re-layouts  7.27 us
    ppermute x1, starting transfers between devices, shifted(): return lax.ppermute(array, axis, pairs)  3.83 us
  transfers between devices with their start and end apart: 7, of which 5 were waited for; matrix products, arithmetic and copies ran while one was open for 14% of the time, Pallas kernels for 0%

profile of v1, /device:TPU:0, one launch (start us, length us, event | category | flops | bytes accessed | tf_op | source)
XLA Modules:
  0.0 165.7 jit_solution(7249064183280385666)
XLA Ops:
  6.5 7.4 %all-to-all-start = ((bf16[8,32,512]{2,1,0:T(8,128)(2,1)}), bf16[8,32,512]{2,1,0:T(8,128)(2,1)}, u32[]{:S(2)}, u32[]{:S(2)}) async-start(bf16[8,32,512]{2,1,0:T(8,128)(2,1)} %bitcast.89), calls=%async_computation | async-start | bytes 524288 | tf_op jit(solution)/shard_map/all_to_all | solution.py:96
  14.1 1.2 compare_and_fusion.1
  15.2 1.0 sort.17
  16.2 0.8 reduce-window.18
  18.6 4.3 %collective-permute-done = bf16[512,512]{1,0:T(8,128)(2,1)S(1)} collective-permute-done((bf16[512,512]{1,0:T(8,128)(2,1)}, bf16[512,512]{1,0:T(8,128)(2,1)S(1)}, u32[]{:S(2)}, u32[]{:S(2)}) %collective-permute-start) | collective-permute-done | bytes 524320 | tf_op jit(solution)/shard_map/ppermute | solution.py:106
  23.0 1.5 gather_fusion
  24.5 0.8 bitcast_select_fusion
  25.4 0.7 broadcast_compare_fusion
  26.7 4.8 %collective-permute-done.1 = bf16[512,512]{1,0:T(8,128)(2,1)S(1)} collective-permute-done((bf16[512,512]{1,0:T(8,128)(2,1)S(1)}, bf16[512,512]{1,0:T(8,128)(2,1)S(1)}, u32[]{:S(2)}, u32[]{:S(2)}) %collective-permute-start.1) | collective-permute-done | bytes 524320 | tf_op jit(solution)/shard_map/ppermute | solution.py:106
  32.2 0.7 constant_dynamic-update-slice_fusion
  33.6 12.1 %collective-permute-done.2 = bf16[512,512]{1,0:T(8,128)(2,1)S(1)} collective-permute-done((bf16[512,512]{1,0:T(8,128)(2,1)S(1)}, bf16[512,512]{1,0:T(8,128)(2,1)S(1)}, u32[]{:S(2)}, u32[]{:S(2)}) %collective-permute-start.2) | collective-permute-done | bytes 524320 | tf_op jit(solution)/shard_map/ppermute | solution.py:106
  45.7 0.8 constant_dynamic-update-slice_fusion.9
  46.5 0.8 constant_dynamic-update-slice_fusion.8
  47.4 0.9 constant_dynamic-update-slice_fusion.7
  48.2 0.8 constant_dynamic-update-slice_fusion.6
  49.1 0.8 constant_dynamic-update-slice_fusion.5
  49.9 0.8 constant_dynamic-update-slice_fusion.4
  50.7 0.8 constant_dynamic-update-slice_fusion.3
  51.6 0.8 constant_dynamic-update-slice_fusion.2
  52.4 2.0 %convolution_convert_fusion.1 = bf16[256,384]{1,0:T(8,128)(2,1)S(1)} fusion(bf16[256,2048]{1,0:T(8,128)(2,1)} %all-gather.5.cloned.1.call-done, bf16[2048,384]{1,0:T(8,128)(2,1)S(1)} %copy-done), kind=kOutput, calls=%fused_computation.18 | convolution fusion | flops 402751488 | bytes 2818048 | tf_op jit(solution)/shard_map/dot_general | solution.py:114
  54.4 2.6 %fusion.16 = bf16[256,512]{1,0:T(8,128)(2,1)S(1)} fusion(bf16[256,2048]{1,0:T(8,128)(2,1)} %all-gather.5.cloned.1.call-done, bf16[4096,512]{1,0:T(8,128)(2,1)} %constant_dynamic-update-slice_fusion.2, s32[]{:T(128)S(6)} %select_n.88), kind=kOutput, calls=%fused_computation.14 | convolution fusion | flops 537001984 | bytes 3407876 | tf_op jit(solution)/shard_map/dot_general | solution.py:114
  57.1 3.8 %collective-permute-start.3 = (bf16[3,896]{1,0:T(4,128)(2,1)S(1)}, bf16[3,896]{1,0:T(4,128)(2,1)S(1)}, u32[]{:S(2)}, u32[]{:S(2)}) collective-permute-start(bf16[3,896]{1,0:T(4,128)(2,1)S(1)} %pad_maximum_fusion), channel_id=1, source_target_pairs={{0,4},{4,8},{8,12},{12,16},{16,20},{20,24},{24,28},{1,5},{5,9},{9,... | collective-permute-start | bytes 16136 | tf_op jit(solution)/shard_map/ppermute | solution.py:12
  61.4 1.8 %reduce-window.19 = f32[6,2,128]{2,1,0:T(2,128)S(1)} reduce-window(f32[6,2,128]{2,1,0:T(2,128)S(1)} %reshape.175, f32[]{:T(128)} %constant.104.clone.1), window={size=1x1x128 pad=0_0x0_0x127_0}, to_apply=%region_3.4 | reduce-window | flops 195072 | bytes 12292 | tf_op jit(solution)/shard_map/reduce-window.1
  63.6 0.8 slice_reduce_fusion
  65.6 1.2 fusion.31
  68.2 0.7 fusion.37
  68.9 19.7 %all-gather.1 = f32[8,1,6]{2,1,0:T(1,128)} all-gather(f32[1,1,6]{2,1,0:T(1,128)S(1)} %bitcast.95), channel_id=1, replica_groups=mesh['seq'=8,'fsdp'=4] {'seq'}, dimensions={0}, use_global_device_ids=true | all-gather | bytes 216 | tf_op jit(solution)/shard_map/all_gather | solution.py:17
  89.1 38.3 %all-gather.7.cloned.1.call-done = f32[48,64,256]{2,1,0:T(8,128)} async-done(((f32[6,64,256]{2,1,0:T(8,128)}), f32[48,64,256]{2,1,0:T(8,128)}) %all-gather.7.cloned.1.call-update) | async-done | bytes 3145744 | tf_op jit(solution)/shard_map/all_gather | solution.py:17
  128.0 2.8 %fusion.13 = f32[256,6,64]{0,2,1:T(8,128)S(1)} fusion(f32[256,6,64]{0,2,1:T(8,128)S(1)} %convolution_multiply_fusion, f32[6,256]{1,0:T(8,128)} %bitcast.92, f32[256,256]{1,0:T(8,128)S(1)} %fusion.39, pred[256,256]{1,0:T(8,128)(4,1)} %fusion.37, f32[256,6,64]{0,2,1:T(8,128)S(1)} %bitcast.85, f32[6]{0:T(128)} %param.25, f32[256,6]{0,1:T(8,128)S(1)} %compare_select_fusion.1), kind=kOutput, calls=%fused_computation.13 | convolution fusion | flops 303562752 | bytes 1519640 | tf_op jit(solution)/shard_map/hts,shp->thp/dot_general | solution.py:60
  130.9 2.5 %multiply_convert_fusion = bf16[256,384]{1,0:T(8,128)(2,1)S(1)} fusion(f32[256,384]{1,0:T(8,128)S(1)} %copy.49, bf16[256,2048]{1,0:T(8,128)(2,1)} %all-gather.5.cloned.1.call-done, bf16[2048,384]{1,0:T(8,128)(2,1)} %param.18), kind=kOutput, calls=%fused_computation.37 | convolution fusion | flops 403439616 | bytes 3211264 | tf_op jit(solution)/shard_map/dot_general | solution.py:114
  133.4 0.7 gather_fusion.1
  134.2 23.9 %all_to_all.10 = bf16[8,32,384]{2,1,0:T(8,128)(2,1)S(1)} all-to-all(bf16[8,32,384]{2,1,0:T(8,128)(2,1)S(1)} %broadcast_select_fusion), channel_id=1, replica_groups=mesh['seq'=8,'fsdp'=4] {'seq'}, dimensions={0} | all-to-all | bytes 393216 | tf_op jit(solution)/shard_map/all_to_all | solution.py:151
  (63 shorter events, 8.3 us)
Async XLA Ops:
  6.5 45.9 %copy-start = (bf16[2048,384]{1,0:T(8,128)(2,1)S(1)}, bf16[2048,384]{1,0:T(8,128)(2,1)}, u32[]{:S(2)}) copy-start(bf16[2048,384]{1,0:T(8,128)(2,1)} %param.17) | copy-start | bytes 4718596
  6.5 41.7 %copy-start.1 = (bf16[512,512]{1,0:T(8,128)(2,1)S(1)}, bf16[512,512]{1,0:T(8,128)(2,1)}, u32[]{:S(2)}) copy-start(bf16[512,512]{1,0:T(8,128)(2,1)} %param.19) | copy-start | bytes 1572868
  6.5 16.4 %all-to-all-start = ((bf16[8,32,512]{2,1,0:T(8,128)(2,1)}), bf16[8,32,512]{2,1,0:T(8,128)(2,1)}, u32[]{:S(2)}, u32[]{:S(2)}) async-start(bf16[8,32,512]{2,1,0:T(8,128)(2,1)} %bitcast.89), calls=%async_computation | async-start | bytes 524288 | tf_op jit(solution)/shard_map/all_to_all | solution.py:96
  14.0 38.5 %all-gather.5.cloned.1.call-start = ((), (), s32[]{:S(2)}) async-start(), calls=%async_computation.2 | async-start | bytes 1310720 | tf_op jit(solution)/shard_map/all_gather | solution.py:111
  14.0 8.9 %collective-permute-start = (bf16[512,512]{1,0:T(8,128)(2,1)}, bf16[512,512]{1,0:T(8,128)(2,1)S(1)}, u32[]{:S(2)}, u32[]{:S(2)}) collective-permute-start(bf16[512,512]{1,0:T(8,128)(2,1)} %param.19), channel_id=1, source_target_pairs={{0,1},{1,2},{2,3},{3,0},{4,5},{5,6},{6,7},{7,4},{8,9},{9,10},{10,1... | collective-permute-start | bytes 1572872 | tf_op jit(solution)/shard_map/ppermute | solution.py:106
  22.9 8.6 %collective-permute-start.1 = (bf16[512,512]{1,0:T(8,128)(2,1)S(1)}, bf16[512,512]{1,0:T(8,128)(2,1)S(1)}, u32[]{:S(2)}, u32[]{:S(2)}) collective-permute-start(bf16[512,512]{1,0:T(8,128)(2,1)S(1)} %collective-permute-done), channel_id=1, source_target_pairs={{0,1},{1,2},{2,3},{3,0},{4,5},{5,6},{6,7},{7,4},{8,9},{9,10},{10,1... | collective-permute-start | bytes 1572872 | tf_op jit(solution)/shard_map/ppermute | solution.py:106
  25.3 102.1 %all-gather.7.cloned.1.call-start = ((), (), s32[]{:S(2)}) async-start(), calls=%async_computation.3 | async-start | bytes 3538944 | tf_op jit(solution)/shard_map/all_gather | solution.py:17
  31.5 14.2 %collective-permute-start.2 = (bf16[512,512]{1,0:T(8,128)(2,1)S(1)}, bf16[512,512]{1,0:T(8,128)(2,1)S(1)}, u32[]{:S(2)}, u32[]{:S(2)}) collective-permute-start(bf16[512,512]{1,0:T(8,128)(2,1)S(1)} %collective-permute-done.1), channel_id=1, source_target_pairs={{0,1},{1,2},{2,3},{3,0},{4,5},{5,6},{6,7},{7,4},{8,9},{9,10},{10,1... | collective-permute-start | bytes 1572872 | tf_op jit(solution)/shard_map/ppermute | solution.py:106
  51.6 9.4 %copy-start.3 = (bf16[2048,6]{0,1:T(8,128)(2,1)S(1)}, bf16[2048,6]{0,1:T(8,128)(2,1)}, u32[]{:S(2)}) copy-start(bf16[2048,6]{0,1:T(8,128)(2,1)} %param.20) | copy-start | bytes 73732
  51.6 9.4 %copy-start.6 = (f32[6]{0:T(128)S(1)}, f32[6]{0:T(128)}, u32[]{:S(2)}) copy-start(f32[6]{0:T(128)} %param.23) | copy-start | bytes 76
  52.4 8.5 %copy-start.2 = (bf16[256,2048]{1,0:T(8,128)(2,1)S(1)}, bf16[256,2048]{1,0:T(8,128)(2,1)}, u32[]{:S(2)}) copy-start(bf16[256,2048]{1,0:T(8,128)(2,1)} %all-gather.5.cloned.1.call-done) | copy-start | bytes 3145732
  57.1 7.5 %collective-permute-start.3 = (bf16[3,896]{1,0:T(4,128)(2,1)S(1)}, bf16[3,896]{1,0:T(4,128)(2,1)S(1)}, u32[]{:S(2)}, u32[]{:S(2)}) collective-permute-start(bf16[3,896]{1,0:T(4,128)(2,1)S(1)} %pad_maximum_fusion), channel_id=1, source_target_pairs={{0,4},{4,8},{8,12},{12,16},{16,20},{20,24},{24,28},{1,5},{5,9},{9,... | collective-permute-start | bytes 16136 | tf_op jit(solution)/shard_map/ppermute | solution.py:12
  63.6 3.2 %copy-start.4 = (f32[1,6,2,128]{3,1,2,0:T(8,128)}, f32[1,6,2,128]{3,1,2,0:T(8,128)S(1)}, u32[]{:S(2)}) copy-start(f32[1,6,2,128]{3,1,2,0:T(8,128)S(1)} %copy.58) | copy-start | bytes 18436
  128.0 6.2 %copy-start.5 = (pred[8]{0:T(512)(128)(4,1)S(1)}, pred[8]{0:T(512)(128)(4,1)}, u32[]{:S(2)}) copy-start(pred[8]{0:T(512)(128)(4,1)} %get-tuple-element.68) | copy-start | bytes 28
Sparse Core Ops, SparseCore 0:
  25.5 21.1 all-gather.4
  67.0 60.4 all-gather.6
